TPU v7x, 32 devices: a whole 2x2x4 slice. The times are simulated.
32 devices in a mesh: blk: 4 (over x, core), rep: 8 (over z, y).
Axes of the slice: x: 2, y: 2, z: 4, core: 2. Of those that a mesh axis runs over, the one named last changes fastest.
Arguments:
- features: bfloat16 [4096, 256], P(('blk', 'rep')), may hold values from -6 to 6
- weight_one: bfloat16 [256, 256], replicated, may hold values from -0.375 to 0.375
- weight_two: bfloat16 [256, 256], replicated, may hold values from -0.375 to 0.375
- tile_values: bfloat16 [4, 8, 24, 128, 128], P('blk', 'rep'), may hold values from -0.125 to 0.125
- tile_rows: int32 [4, 8, 24], P('blk', 'rep'), may hold values from 0 to 7, as said below
- tile_cols: int32 [4, 8, 24], P('blk', 'rep'), may hold values from 0 to 31, as said below
- tile_count: int32 [4, 8], P('blk', 'rep'), may hold values from 16 to 24, as said below
Outputs:
- aggregated: bfloat16 [4096, 256], P(('blk', 'rep'))
Inputs may be any that keep to these rules, and one draw needn't show every extreme that they name: `tile_rows`: block row within the holder's row group into which a tile adds; slots k >= tile_count are ignored. `tile_cols`: A tile held at rep index r has column block j * 8 + r for some j: its columns are nodes held by a device of rep index r. `tile_count`: one device holds exactly 24 live tiles.
All inputs are finite; a program needn't handle non-finite values.
Results may differ from a plain program's by a relative error of at most 0.035.
Values may be sent and summed in bfloat16 or wider, within the bound.
No kernel may reach another device: no remote copies, remote signals or barrier semaphores. Data moves between devices by JAX's collectives and lax.ppermute only.
A program may use at most 64 MiB of HBM per device.

v0:
```python
import jax
import jax.numpy as jnp
from jax import lax
from jax.sharding import PartitionSpec as P


def tile_products(panel_rows, tile_vals, local_block, block_size, feat_width):
    gathered = lax.all_gather(panel_rows, "blk", axis=0, tiled=True)
    source = gathered.reshape(-1, block_size, feat_width)[local_block]
    return jnp.einsum("kab,kbf->kaf", tile_vals, source, preferred_element_type=jnp.float32)


def body(features, weight_one, weight_two, tile_values, tile_rows, tile_cols, tile_count):
    tile_vals = tile_values[0, 0]
    tile_row = tile_rows[0, 0]
    tile_col = tile_cols[0, 0]
    live_count = tile_count[0, 0]
    feat_width = features.shape[1]
    block_size = tile_vals.shape[-1]
    rows_dev = features.shape[0]
    sub_blocks = rows_dev // block_size
    replicas = lax.axis_size("rep")
    group_blocks = sub_blocks * replicas
    tile_slots = tile_vals.shape[0]
    local_block = tile_col // (replicas * sub_blocks) * sub_blocks + tile_col % sub_blocks
    is_live = (lax.iota(jnp.int32, tile_slots) < live_count).astype(jnp.float32)
    hidden = features
    result = features
    for layer_id in range(2):
        weight = weight_one if layer_id == 0 else weight_two
        panel_rows = jnp.dot(hidden, weight, preferred_element_type=jnp.float32).astype(
            jnp.bfloat16
        )
        products = tile_products(panel_rows, tile_vals, local_block, block_size, feat_width)
        masked = products * is_live[:, None, None]
        partial_value = jax.ops.segment_sum(masked, tile_row, num_segments=group_blocks)
        partial_value = partial_value.astype(jnp.bfloat16).astype(jnp.float32)
        partial_value = partial_value.reshape(group_blocks * block_size, feat_width)
        group_sum = lax.psum(partial_value.astype(jnp.bfloat16), "rep").astype(jnp.float32)
        row_start = lax.axis_index("rep") * rows_dev
        summed = lax.dynamic_slice_in_dim(group_sum, row_start, rows_dev, 0)
        if layer_id == 0:
            hidden = jnp.maximum(summed, 0.0).astype(jnp.bfloat16)
        else:
            result = summed.astype(jnp.bfloat16)
    return result


def solution(mesh):
    in_specs = (
        P(("blk", "rep"), None),
        P(),
        P(),
        P("blk", "rep", None, None, None),
        P("blk", "rep", None),
        P("blk", "rep", None),
        P("blk", "rep"),
    )
    out_specs = P(("blk", "rep"), None)
    return jax.shard_map(body, mesh=mesh, in_specs=in_specs, out_specs=out_specs, check_vma=False)
```

profile of v0, /device:TPU:0, one launch (start us, length us, event | category | flops | bytes accessed | tf_op | source)
XLA Modules:
  0.0 204.6 jit_solution(6900066142206333216)
XLA Ops:
  6.5 0.0 copy-start
  6.5 0.0 all-reduce.3.cloned.1.call-start
  6.5 0.7 fusion.4
  7.3 1.1 convolution_convert_fusion.1
  8.4 7.2 %all_gather.6 = bf16[512,256]{1,0:T(8,128)(2,1)S(1)} all-gather(bf16[128,256]{1,0:T(8,128)(2,1)S(1)} %convolution_convert_fusion.1), channel_id=1, replica_groups=mesh['blk'=4,'rep'=8] {'blk'}, dimensions={0}, use_global_device_ids=true | all-gather | bytes 327680 | tf_op jit(solution)/shard_map/all_gather | solution.py:8
  16.3 0.6 gather_fusion
  16.9 0.0 copy-done
  16.9 2.4 %multiply_bitcast_fusion.1 = f32[24,128,256]{1,2,0:T(8,128)} fusion(bf16[24,128,256]{2,1,0:T(8,128)(2,1)S(1)} %gather_fusion, f32[24]{0:T(128)S(1)} %compare_convert_fusion, bf16[1,1,24,128,128]{4,3,2,1,0:T(8,128)(2,1)S(1)} %copy-done), kind=kOutput, calls=%fused_computation.5 | convolution fusion | flops 202113024 | bytes 5505120 | tf_op jit(solution)/shard_map/kab,kbf->kaf/dot_general | solution.py:10
  19.3 0.0 copy-start.2
  19.3 3.6 %copy.11 = f32[24,128,256]{2,1,0:T(8,128)} copy(f32[24,128,256]{1,2,0:T(8,128)} %multiply_bitcast_fusion.1) | data formatting | bytes 6291456 | tf_op jit(solution)/shard_map/mul | solution.py:35
  22.9 0.1 broadcast.95.clone
  23.0 0.0 copy-done.2
  23.0 0.0 copy-start.1
  23.0 6.1 %scatter_fusion = f32[8,128,256]{2,1,0:T(8,128)S(1)} fusion(f32[8,128,256]{2,1,0:T(8,128)S(1)} %broadcast.95.clone, s32[24]{0:T(128)S(1)} %bitcast.37, f32[24,128,256]{2,1,0:T(8,128)} %copy.11), kind=kCustom, calls=%fused_computation.2 | custom fusion | flops 786432 | bytes 9437280 | tf_op jit(solution)/shard_map/scatter-add | solution.py:36
  29.1 0.9 convert_element_type.43
  30.0 0.0 all-reduce.3.cloned.1.call-update
  30.0 0.0 all-reduce.5.cloned.1.call-start
  30.1 73.8 %all-reduce.3.cloned.1.call-done = bf16[1024,256]{1,0:T(8,128)(2,1)} async-done(((bf16[1024,256]{1,0:T(8,128)(2,1)}), bf16[1024,256]{1,0:T(8,128)(2,1)}) %all-reduce.3.cloned.1.call-update) | async-done | bytes 524304 | tf_op jit(solution)/shard_map/psum | solution.py:39
  103.9 0.0 copy-done.1
  103.9 1.0 convolution_convert_fusion
  104.9 5.8 %all_gather.7 = bf16[512,256]{1,0:T(8,128)(2,1)S(1)} all-gather(bf16[128,256]{1,0:T(8,128)(2,1)S(1)} %convolution_convert_fusion), channel_id=1, replica_groups=mesh['blk'=4,'rep'=8] {'blk'}, dimensions={0}, use_global_device_ids=true | all-gather | bytes 327680 | tf_op jit(solution)/shard_map/all_gather | solution.py:8
  110.7 0.6 gather_fusion.1
  111.3 2.4 %multiply_bitcast_fusion = f32[24,128,256]{1,2,0:T(8,128)} fusion(bf16[24,128,256]{2,1,0:T(8,128)(2,1)S(1)} %gather_fusion.1, f32[24]{0:T(128)S(1)} %compare_convert_fusion, bf16[1,1,24,128,128]{4,3,2,1,0:T(8,128)(2,1)S(1)} %copy-done), kind=kOutput, calls=%fused_computation.4 | convolution fusion | flops 202113024 | bytes 5505120 | tf_op jit(solution)/shard_map/kab,kbf->kaf/dot_general | solution.py:10
  113.7 3.6 %copy.13 = f32[24,128,256]{2,1,0:T(8,128)} copy(f32[24,128,256]{1,2,0:T(8,128)} %multiply_bitcast_fusion) | data formatting | bytes 6291456 | tf_op jit(solution)/shard_map/mul | solution.py:35
  117.3 0.1 broadcast.95
  117.4 6.1 %scatter_fusion.1 = f32[8,128,256]{2,1,0:T(8,128)S(1)} fusion(f32[8,128,256]{2,1,0:T(8,128)S(1)} %broadcast.95, s32[24]{0:T(128)S(1)} %bitcast.38, f32[24,128,256]{2,1,0:T(8,128)} %copy.13), kind=kCustom, calls=%fused_computation.3 | custom fusion | flops 786432 | bytes 9437280 | tf_op jit(solution)/shard_map/scatter-add | solution.py:36
  123.5 0.9 convert_element_type.48
  124.4 0.0 all-reduce.5.cloned.1.call-update
  124.4 71.9 %all-reduce.5.cloned.1.call-done = bf16[1024,256]{1,0:T(8,128)(2,1)} async-done(((bf16[1024,256]{1,0:T(8,128)(2,1)}), bf16[1024,256]{1,0:T(8,128)(2,1)}) %all-reduce.5.cloned.1.call-update) | async-done | bytes 524304 | tf_op jit(solution)/shard_map/psum | solution.py:39
  196.3 1.5 convert_convert_fusion
  (2 shorter events, 0.0 us)
Async XLA Ops:
  6.5 10.4 %copy-start = (bf16[1,1,24,128,128]{4,3,2,1,0:T(8,128)(2,1)S(1)}, bf16[1,1,24,128,128]{4,3,2,1,0:T(8,128)(2,1)}, u32[]{:S(2)}) copy-start(bf16[1,1,24,128,128]{4,3,2,1,0:T(8,128)(2,1)} %param.10) | copy-start | bytes 2359300
  6.5 97.4 %all-reduce.3.cloned.1.call-start = ((), (), s32[]{:S(2)}) async-start(), calls=%async_computation | async-start | bytes 1048576 | tf_op jit(solution)/shard_map/psum | solution.py:39
  19.3 3.7 %copy-start.2 = (s32[1,1,24]{2,1,0:T(1,128)S(1)}, s32[1,1,24]{2,1,0:T(1,128)}, u32[]{:S(2)}) copy-start(s32[1,1,24]{2,1,0:T(1,128)} %param.11) | copy-start | bytes 292
  23.0 80.9 %copy-start.1 = (bf16[256,256]{1,0:T(8,128)(2,1)S(1)}, bf16[256,256]{1,0:T(8,128)(2,1)}, u32[]{:S(2)}) copy-start(bf16[256,256]{1,0:T(8,128)(2,1)} %param.9) | copy-start | bytes 393220
  30.0 166.2 %all-reduce.5.cloned.1.call-start = ((), (), s32[]{:S(2)}) async-start(), calls=%async_computation.1 | async-start | bytes 1048576 | tf_op jit(solution)/shard_map/psum | solution.py:39
Sparse Core Ops, SparseCore 0:
  30.1 73.7 all-reduce.2
  124.5 71.6 all-reduce.4
where the time goes:
time: 205 us
  waiting for transfers between devices  146 us (71%)
  other arithmetic  16.1 us (8%)
  between operations  14.2 us (7%)
  blocking collectives  13 us (6%)
  local copies, waits for them, and re-layouts  8.65 us (4%)
  matrix products  6.9 us (3%)
    psum x2, waiting for transfers between devices, body(): lax.psum(partial_value.astype(jnp.bfloat16), 'rep').astype(jnp.float32)  146 us
    all_gather x2, blocking collectives, tile_products(): gathered = lax.all_gather(panel_rows, 'blk', axis=0, tiled=True)  13 us
    scatter-add x2, other arithmetic, body(): jax.ops.segment_sum(masked, tile_row, num_segments=group_blocks)  12.2 us
    mul x2, local copies, waits for them, and re-layouts, body(): masked = products * is_live[:, None, None]  7.18 us
    dot_general x2, matrix products, tile_products(): jnp.einsum('kab,kbf->kaf', tile_vals, source, preferred_element_type=jnp....  4.8 us
  transfers between devices with their start and end apart: 2, of which 2 were waited for; matrix products, arithmetic and copies ran while one was open for 0% of the time, Pallas kernels for 0%

commit v1 on v0

--- a/solution.py
+++ b/solution.py
@@ -5,7 +5,12 @@
 
 
 def tile_products(panel_rows, tile_vals, local_block, block_size, feat_width):
-    gathered = lax.all_gather(panel_rows, "blk", axis=0, tiled=True)
+    ring = [panel_rows]
+    for hop in range(3):
+        ring.append(lax.ppermute(ring[-1], "blk", [(dev, (dev + 1) % 4) for dev in range(4)]))
+    gathered = jnp.roll(
+        jnp.concatenate(ring[::-1], axis=0), (lax.axis_index("blk") + 1) * ring[0].shape[0], axis=0
+    )
     source = gathered.reshape(-1, block_size, feat_width)[local_block]
     return jnp.einsum("kab,kbf->kaf", tile_vals, source, preferred_element_type=jnp.float32)
 

time: 205 us -> 219 us (1.068)
  waiting for transfers between devices: 146 us -> 167 us
  blocking collectives: 13 us -> 0 us
  other arithmetic: 16.1 us -> 20.7 us
    ppermute x0 -> x6, waiting for transfers between devices: none -> 20.8 us  [tile_products(): lax.ppermute(ring[-1], 'blk', [(dev, (dev + 1) % 4) for dev in range(4)])]
    all_gather x2 -> x0, blocking collectives: 13 us -> none  [tile_products(): gathered = lax.all_gather(panel_rows, 'blk', axis=0, tiled=True)]
    concatenate x0 -> x2, other arithmetic: none -> 4.64 us  [tile_products(): jnp.roll(jnp.concatenate(ring[::-1], axis=0), (lax.axis_index('blk') + 1)...]
  transfers between devices with their start and end apart: 2 -> 8, of which waited for: 2 -> 8; matrix products, arithmetic and copies ran while one was open for 0% -> 0% of each run, Pallas kernels for 0% -> 0%
where the time goes in v1:
time: 219 us; the launch traced here: 218 us
  waiting for transfers between devices  167 us (76%)
  other arithmetic  20.7 us (9%)
  between operations  14.2 us (6%)
  local copies, waits for them, and re-layouts  8.57 us (4%)
  matrix products  6.92 us (3%)
    psum x2, waiting for transfers between devices, body(): lax.psum(partial_value.astype(jnp.bfloat16), 'rep').astype(jnp.float32)  146 us
    ppermute x6, waiting for transfers between devices, tile_products(): lax.ppermute(ring[-1], 'blk', [(dev, (dev + 1) % 4) for dev in range(4)])  20.8 us
    scatter-add x2, other arithmetic, body(): jax.ops.segment_sum(masked, tile_row, num_segments=group_blocks)  12.2 us
    mul x2, local copies, waits for them, and re-layouts, body(): masked = products * is_live[:, None, None]  7.1 us
    dot_general x2, matrix products, tile_products(): jnp.einsum('kab,kbf->kaf', tile_vals, source, preferred_element_type=jnp....  4.76 us
    concatenate x2, other arithmetic, tile_products(): jnp.roll(jnp.concatenate(ring[::-1], axis=0), (lax.axis_index('blk') + 1)...  4.64 us
  transfers between devices with their start and end apart: 8, of which 8 were waited for; matrix products, arithmetic and copies ran while one was open for 0% of the time, Pallas kernels for 0%

profile of v1, /device:TPU:0, one launch (start us, length us, event | category | flops | bytes accessed | tf_op | source)
XLA Modules:
  0.0 218.3 jit_solution(18236405285620745412)
XLA Ops:
  6.5 0.0 copy-start
  6.5 0.0 all-reduce.3.cloned.1.call-start
  6.5 1.2 convolution_convert_fusion.1
  7.7 0.5 collective-permute-start
  8.2 0.7 fusion.19
  9.5 2.6 %collective-permute-done = bf16[128,256]{1,0:T(8,128)(2,1)S(1)} collective-permute-done((bf16[128,256]{1,0:T(8,128)(2,1)S(1)}, bf16[128,256]{1,0:T(8,128)(2,1)S(1)}, u32[]{:S(2)}, u32[]{:S(2)}) %collective-permute-start) | collective-permute-done | bytes 65568 | tf_op jit(solution)/shard_map/ppermute | solution.py:10
  12.1 0.1 collective-permute-start.1
  12.2 3.6 %collective-permute-done.1 = bf16[128,256]{1,0:T(8,128)(2,1)S(1)} collective-permute-done((bf16[128,256]{1,0:T(8,128)(2,1)S(1)}, bf16[128,256]{1,0:T(8,128)(2,1)S(1)}, u32[]{:S(2)}, u32[]{:S(2)}) %collective-permute-start.1) | collective-permute-done | bytes 65568 | tf_op jit(solution)/shard_map/ppermute | solution.py:10
  15.8 0.1 collective-permute-start.2
  15.8 3.6 %collective-permute-done.2 = bf16[128,256]{1,0:T(8,128)(2,1)S(1)} collective-permute-done((bf16[128,256]{1,0:T(8,128)(2,1)S(1)}, bf16[128,256]{1,0:T(8,128)(2,1)S(1)}, u32[]{:S(2)}, u32[]{:S(2)}) %collective-permute-start.2) | collective-permute-done | bytes 65568 | tf_op jit(solution)/shard_map/ppermute | solution.py:10
  19.5 2.3 %fusion.12 = bf16[512,256]{1,0:T(8,128)(2,1)S(1)} fusion(s32[]{:T(128)S(6)} %select_n.48, bf16[128,256]{1,0:T(8,128)(2,1)S(1)} %collective-permute-done.2, bf16[128,256]{1,0:T(8,128)(2,1)S(1)} %collective-permute-done.1, bf16[128,256]{1,0:T(8,128)(2,1)S(1)} %collective-permute-done, bf16[128,256]{1,0:T(8,128)(2,1)S(1)} %convolution_convert_fusion.1), kind=kLoop, calls=%fused_computation.36 | loop fusion | flops 2097152 | bytes 524292 | tf_op jit(solution)/shard_map/jit(_roll_dynamic)/concatenate | solution.py:11
  21.8 0.6 gather_fusion
  22.5 0.0 copy-done
  22.5 2.4 %multiply_bitcast_fusion.1 = f32[24,128,256]{1,2,0:T(8,128)} fusion(bf16[24,128,256]{2,1,0:T(8,128)(2,1)S(1)} %gather_fusion, f32[24]{0:T(128)S(1)} %compare_convert_fusion, bf16[1,1,24,128,128]{4,3,2,1,0:T(8,128)(2,1)S(1)} %copy-done), kind=kOutput, calls=%fused_computation.5 | convolution fusion | flops 202113024 | bytes 5505120 | tf_op jit(solution)/shard_map/kab,kbf->kaf/dot_general | solution.py:15
  24.9 0.0 copy-start.2
  24.9 3.6 %copy.11 = f32[24,128,256]{2,1,0:T(8,128)} copy(f32[24,128,256]{1,2,0:T(8,128)} %multiply_bitcast_fusion.1) | data formatting | bytes 6291456 | tf_op jit(solution)/shard_map/mul | solution.py:40
  28.4 0.1 broadcast.96.clone
  28.5 0.0 copy-done.2
  28.5 0.0 copy-start.1
  28.5 6.1 %scatter_fusion = f32[8,128,256]{2,1,0:T(8,128)S(1)} fusion(f32[8,128,256]{2,1,0:T(8,128)S(1)} %broadcast.96.clone, s32[24]{0:T(128)S(1)} %bitcast.37, f32[24,128,256]{2,1,0:T(8,128)} %copy.11), kind=kCustom, calls=%fused_computation.2 | custom fusion | flops 786432 | bytes 9437280 | tf_op jit(solution)/shard_map/scatter-add | solution.py:41
  34.6 0.8 convert_element_type.43
  35.5 0.0 all-reduce.3.cloned.1.call-update
  35.5 0.0 all-reduce.5.cloned.1.call-start
  35.5 74.6 %all-reduce.3.cloned.1.call-done = bf16[1024,256]{1,0:T(8,128)(2,1)} async-done(((bf16[1024,256]{1,0:T(8,128)(2,1)}), bf16[1024,256]{1,0:T(8,128)(2,1)}) %all-reduce.3.cloned.1.call-update) | async-done | bytes 524304 | tf_op jit(solution)/shard_map/psum | solution.py:44
  110.1 0.0 copy-done.1
  110.1 1.0 convolution_convert_fusion
  111.1 0.1 collective-permute-start.3
  111.2 3.7 %collective-permute-done.3 = bf16[128,256]{1,0:T(8,128)(2,1)S(1)} collective-permute-done((bf16[128,256]{1,0:T(8,128)(2,1)S(1)}, bf16[128,256]{1,0:T(8,128)(2,1)S(1)}, u32[]{:S(2)}, u32[]{:S(2)}) %collective-permute-start.3) | collective-permute-done | bytes 65568 | tf_op jit(solution)/shard_map/ppermute | solution.py:10
  114.9 0.0 collective-permute-start.4
  114.9 3.7 %collective-permute-done.4 = bf16[128,256]{1,0:T(8,128)(2,1)S(1)} collective-permute-done((bf16[128,256]{1,0:T(8,128)(2,1)S(1)}, bf16[128,256]{1,0:T(8,128)(2,1)S(1)}, u32[]{:S(2)}, u32[]{:S(2)}) %collective-permute-start.4) | collective-permute-done | bytes 65568 | tf_op jit(solution)/shard_map/ppermute | solution.py:10
  118.5 0.0 collective-permute-start.5
  118.6 3.7 %collective-permute-done.5 = bf16[128,256]{1,0:T(8,128)(2,1)S(1)} collective-permute-done((bf16[128,256]{1,0:T(8,128)(2,1)S(1)}, bf16[128,256]{1,0:T(8,128)(2,1)S(1)}, u32[]{:S(2)}, u32[]{:S(2)}) %collective-permute-start.5) | collective-permute-done | bytes 65568 | tf_op jit(solution)/shard_map/ppermute | solution.py:10
  122.2 2.3 %fusion.5 = bf16[512,256]{1,0:T(8,128)(2,1)S(1)} fusion(s32[]{:T(128)S(6)} %select_n.48, bf16[128,256]{1,0:T(8,128)(2,1)S(1)} %collective-permute-done.5, bf16[128,256]{1,0:T(8,128)(2,1)S(1)} %collective-permute-done.4, bf16[128,256]{1,0:T(8,128)(2,1)S(1)} %collective-permute-done.3, bf16[128,256]{1,0:T(8,128)(2,1)S(1)} %convolution_convert_fusion), kind=kLoop, calls=%fused_computation.29 | loop fusion | flops 2097152 | bytes 524292 | tf_op jit(solution)/shard_map/jit(_roll_dynamic)/concatenate | solution.py:11
  124.6 0.6 gather_fusion.1
  125.2 2.4 %multiply_bitcast_fusion = f32[24,128,256]{1,2,0:T(8,128)} fusion(bf16[24,128,256]{2,1,0:T(8,128)(2,1)S(1)} %gather_fusion.1, f32[24]{0:T(128)S(1)} %compare_convert_fusion, bf16[1,1,24,128,128]{4,3,2,1,0:T(8,128)(2,1)S(1)} %copy-done), kind=kOutput, calls=%fused_computation.4 | convolution fusion | flops 202113024 | bytes 5505120 | tf_op jit(solution)/shard_map/kab,kbf->kaf/dot_general | solution.py:15
  127.6 3.5 %copy.13 = f32[24,128,256]{2,1,0:T(8,128)} copy(f32[24,128,256]{1,2,0:T(8,128)} %multiply_bitcast_fusion) | data formatting | bytes 6291456 | tf_op jit(solution)/shard_map/mul | solution.py:40
  131.1 0.1 broadcast.96
  131.2 6.1 %scatter_fusion.1 = f32[8,128,256]{2,1,0:T(8,128)S(1)} fusion(f32[8,128,256]{2,1,0:T(8,128)S(1)} %broadcast.96, s32[24]{0:T(128)S(1)} %bitcast.38, f32[24,128,256]{2,1,0:T(8,128)} %copy.13), kind=kCustom, calls=%fused_computation.3 | custom fusion | flops 786432 | bytes 9437280 | tf_op jit(solution)/shard_map/scatter-add | solution.py:41
  137.3 0.8 convert_element_type.48
  138.2 0.0 all-reduce.5.cloned.1.call-update
  138.2 71.8 %all-reduce.5.cloned.1.call-done = bf16[1024,256]{1,0:T(8,128)(2,1)} async-done(((bf16[1024,256]{1,0:T(8,128)(2,1)}), bf16[1024,256]{1,0:T(8,128)(2,1)}) %all-reduce.5.cloned.1.call-update) | async-done | bytes 524304 | tf_op jit(solution)/shard_map/psum | solution.py:44
  210.0 1.5 convert_convert_fusion
  (2 shorter events, 0.0 us)
Async XLA Ops:
  6.5 15.9 %copy-start = (bf16[1,1,24,128,128]{4,3,2,1,0:T(8,128)(2,1)S(1)}, bf16[1,1,24,128,128]{4,3,2,1,0:T(8,128)(2,1)}, u32[]{:S(2)}) copy-start(bf16[1,1,24,128,128]{4,3,2,1,0:T(8,128)(2,1)} %param.12) | copy-start | bytes 2359300
  6.5 103.6 %all-reduce.3.cloned.1.call-start = ((), (), s32[]{:S(2)}) async-start(), calls=%async_computation | async-start | bytes 1048576 | tf_op jit(solution)/shard_map/psum | solution.py:44
  7.7 4.4 %collective-permute-start = (bf16[128,256]{1,0:T(8,128)(2,1)S(1)}, bf16[128,256]{1,0:T(8,128)(2,1)S(1)}, u32[]{:S(2)}, u32[]{:S(2)}) collective-permute-start(bf16[128,256]{1,0:T(8,128)(2,1)S(1)} %convolution_convert_fusion.1), channel_id=1, source_target_pairs={{0,8},{8,16},{16,24},{24,0},{1,9},{9,17},{17,25},{25,1},{2,10},{10... | collective-permute-start | bytes 196616 | tf_op jit(solution)/shard_map/ppermute | solution.py:10
  12.1 3.7 %collective-permute-start.1 = (bf16[128,256]{1,0:T(8,128)(2,1)S(1)}, bf16[128,256]{1,0:T(8,128)(2,1)S(1)}, u32[]{:S(2)}, u32[]{:S(2)}) collective-permute-start(bf16[128,256]{1,0:T(8,128)(2,1)S(1)} %collective-permute-done), channel_id=1, source_target_pairs={{0,8},{8,16},{16,24},{24,0},{1,9},{9,17},{17,25},{25,1},{2,10},{10... | collective-permute-start | bytes 196616 | tf_op jit(solution)/shard_map/ppermute | solution.py:10
  15.8 3.7 %collective-permute-start.2 = (bf16[128,256]{1,0:T(8,128)(2,1)S(1)}, bf16[128,256]{1,0:T(8,128)(2,1)S(1)}, u32[]{:S(2)}, u32[]{:S(2)}) collective-permute-start(bf16[128,256]{1,0:T(8,128)(2,1)S(1)} %collective-permute-done.1), channel_id=1, source_target_pairs={{0,8},{8,16},{16,24},{24,0},{1,9},{9,17},{17,25},{25,1},{2,10},{10... | collective-permute-start | bytes 196616 | tf_op jit(solution)/shard_map/ppermute | solution.py:10
  24.9 3.6 %copy-start.2 = (s32[1,1,24]{2,1,0:T(1,128)S(1)}, s32[1,1,24]{2,1,0:T(1,128)}, u32[]{:S(2)}) copy-start(s32[1,1,24]{2,1,0:T(1,128)} %param.13) | copy-start | bytes 292
  28.5 81.6 %copy-start.1 = (bf16[256,256]{1,0:T(8,128)(2,1)S(1)}, bf16[256,256]{1,0:T(8,128)(2,1)}, u32[]{:S(2)}) copy-start(bf16[256,256]{1,0:T(8,128)(2,1)} %param.11) | copy-start | bytes 393220
  35.5 174.5 %all-reduce.5.cloned.1.call-start = ((), (), s32[]{:S(2)}) async-start(), calls=%async_computation.1 | async-start | bytes 1048576 | tf_op jit(solution)/shard_map/psum | solution.py:44
  111.1 3.7 %collective-permute-start.3 = (bf16[128,256]{1,0:T(8,128)(2,1)S(1)}, bf16[128,256]{1,0:T(8,128)(2,1)S(1)}, u32[]{:S(2)}, u32[]{:S(2)}) collective-permute-start(bf16[128,256]{1,0:T(8,128)(2,1)S(1)} %convolution_convert_fusion), channel_id=1, source_target_pairs={{0,8},{8,16},{16,24},{24,0},{1,9},{9,17},{17,25},{25,1},{2,10},{10... | collective-permute-start | bytes 196616 | tf_op jit(solution)/shard_map/ppermute | solution.py:10
  114.9 3.7 %collective-permute-start.4 = (bf16[128,256]{1,0:T(8,128)(2,1)S(1)}, bf16[128,256]{1,0:T(8,128)(2,1)S(1)}, u32[]{:S(2)}, u32[]{:S(2)}) collective-permute-start(bf16[128,256]{1,0:T(8,128)(2,1)S(1)} %collective-permute-done.3), channel_id=1, source_target_pairs={{0,8},{8,16},{16,24},{24,0},{1,9},{9,17},{17,25},{25,1},{2,10},{10... | collective-permute-start | bytes 196616 | tf_op jit(solution)/shard_map/ppermute | solution.py:10
  118.5 3.7 %collective-permute-start.5 = (bf16[128,256]{1,0:T(8,128)(2,1)S(1)}, bf16[128,256]{1,0:T(8,128)(2,1)S(1)}, u32[]{:S(2)}, u32[]{:S(2)}) collective-permute-start(bf16[128,256]{1,0:T(8,128)(2,1)S(1)} %collective-permute-done.4), channel_id=1, source_target_pairs={{0,8},{8,16},{16,24},{24,0},{1,9},{9,17},{17,25},{25,1},{2,10},{10... | collective-permute-start | bytes 196616 | tf_op jit(solution)/shard_map/ppermute | solution.py:10
Sparse Core Ops, SparseCore 0:
  35.6 74.4 all-reduce.2
  138.3 71.6 all-reduce.4
